TPU v7x, 32 devices: a whole 2x2x4 slice. The times are simulated.
32 devices in a mesh: req: 4 (over x, core), head: 8 (over z, y).
Axes of the slice: x: 2, y: 2, z: 4, core: 2. Of those that a mesh axis runs over, the one named last changes fastest.
Arguments:
- stretch_acts: bfloat16 [8, 256, 2048], P(None, ('req', 'head')), may hold values from -6 to 6
- cache_prefill: bfloat16 [8, 8, 256, 32, 128], P('req', None, 'head'), may hold values from -600 to 600
- stretch_lens: int32 [8], replicated, may hold values from 1 to 256, 1280 in all
- prefix_lens: int32 [8], replicated, may hold values from 1 to 256, 1280 in all
- req_order: int32 [8], replicated, may hold values from 0 to 7, each once
- attn_gain: bfloat16 [2048], replicated, may hold values from 0.25 to 1.75
- in_weight: bfloat16 [2048, 32, 192], P(None, 'head'), may hold values from -0.125 to 0.125
- slopes: float32 [32], P('head'), may hold values from 0.00390625 to 0.5
- out_weight: bfloat16 [32, 64, 2048], P('head'), may hold values from -0.125 to 0.125
- mlp_gain: bfloat16 [2048], replicated, may hold values from 0.25 to 1.75
- up_weight: bfloat16 [2048, 8192], P(None, 'head'), may hold values from -0.125 to 0.125
- down_weight: bfloat16 [8192, 2048], P('head'), may hold values from -0.0625 to 0.0625
Outputs:
- layer_out: bfloat16 [8, 256, 2048], P(None, ('req', 'head'))
- cache_decode: bfloat16 [8, 8, 256, 32, 128], P(None, 'req', None, 'head')
Inputs may be any that keep to these rules, and one draw needn't show every extreme that they name: `stretch_lens`: the entries sum to 1280 and the largest is exactly 256. `prefix_lens`: the entries sum to 1280 and the largest is exactly 256. `req_order`: each request appears once.
All inputs are finite; a program needn't handle non-finite values.
Results may differ from a plain program's by a relative error of at most 0.013.
The roundings to bfloat16 on the way count: a program that leaves them out, or rounds other values in their place, can miss the bound.
Values may be sent and summed in bfloat16 or wider, within the bound.
No kernel may reach another device: no remote copies, remote signals or barrier semaphores. Data moves between devices by JAX's collectives and lax.ppermute only.
A program may use at most 128 MiB of HBM per device.

v0:
```python
import math
import jax
import jax.numpy as jnp
from jax import lax
from jax.sharding import PartitionSpec as P

EPSILON = 1e-05


def layer_norm(values, gain):
    average = jnp.mean(values, axis=-1, keepdims=True)
    centred = values - average
    variance = jnp.mean(centred * centred, axis=-1, keepdims=True)
    return centred * lax.rsqrt(variance + EPSILON) * gain.astype(jnp.float32)


def attend(queries, pairs, prefix_len, slopes, head_dim):
    stretch = queries.shape[0]
    prefix = pairs.shape[0] - stretch
    keys_part = pairs[..., :head_dim]
    values_part = pairs[..., head_dim:]
    scores = jnp.einsum("qhd,khd->hqk", queries, keys_part, preferred_element_type=jnp.float32) * (
        1.0 / math.sqrt(head_dim)
    )
    row_index = jnp.arange(stretch, dtype=jnp.int32)
    key_index = jnp.arange(prefix + stretch, dtype=jnp.int32)
    in_prefix = key_index < prefix
    query_pos = prefix_len + row_index
    key_pos = jnp.where(in_prefix, key_index, prefix_len + key_index - prefix)
    allowed = jnp.where(
        in_prefix[None, :],
        key_index[None, :] < prefix_len,
        (key_index - prefix)[None, :] <= row_index[:, None],
    )
    distance = (query_pos[:, None] - key_pos[None, :]).astype(jnp.float32)
    scores = scores - slopes[:, None, None] * distance[None]
    scores = jnp.where(allowed[None], scores, -jnp.inf)
    highest = jnp.max(scores, axis=-1, keepdims=True)
    expo = jnp.exp(scores - highest)
    soft = (expo / jnp.sum(expo, axis=-1, keepdims=True)).astype(jnp.bfloat16)
    context = jnp.einsum("hqk,khd->qhd", soft, values_part, preferred_element_type=jnp.float32)
    return context.astype(jnp.bfloat16).reshape(stretch, -1)


def local(
    stretch_acts,
    cache_prefill,
    stretch_lens,
    prefix_lens,
    req_order,
    attn_gain,
    in_weight,
    slopes,
    out_weight,
    mlp_gain,
    up_weight,
    down_weight,
):
    req_count = lax.axis_size("req")
    head_count = lax.axis_size("head")
    req_index = lax.axis_index("req")
    head_index = lax.axis_index("head")
    requests = stretch_acts.shape[0]
    stretch_rows = stretch_acts.shape[1]
    features = stretch_acts.shape[2]
    group_size = requests // req_count
    span_rows = head_count * stretch_rows
    stretch_max = req_count * span_rows
    prefix_rows = cache_prefill.shape[2]
    heads_here = in_weight.shape[1]
    pair_width = cache_prefill.shape[4]
    head_dim = pair_width // 2
    members = lax.dynamic_slice_in_dim(req_order, req_index * group_size, group_size)
    member_stretch = jnp.take(stretch_lens, members)
    member_prefix = jnp.take(prefix_lens, members)
    ordered_prefix = jnp.take(prefix_lens, req_order)
    positions = head_index * prefix_rows + jnp.arange(prefix_rows, dtype=jnp.int32)
    keep = positions[None, :] < ordered_prefix[:, None]
    dealt_cache = jnp.where(
        keep[None, :, :, None, None],
        jnp.take(cache_prefill, req_order, axis=1),
        jnp.zeros((), cache_prefill.dtype),
    )
    relaid = lax.all_to_all(
        lax.all_to_all(dealt_cache, "head", split_axis=3, concat_axis=2, tiled=True),
        "req",
        split_axis=1,
        concat_axis=0,
        tiled=True,
    )
    current = relaid[0]
    dealt_acts = jnp.take(stretch_acts, req_order, axis=0)
    dealt_rows = lax.all_to_all(dealt_acts, "req", split_axis=0, concat_axis=1, tiled=True).reshape(
        group_size, req_count, stretch_rows, features
    )
    gathered = lax.all_gather(dealt_rows, "head", axis=2, tiled=True)
    normed = (
        layer_norm(gathered.astype(jnp.float32), attn_gain)
        .astype(jnp.bfloat16)
        .reshape(group_size * stretch_max, features)
    )
    mixed = jnp.dot(
        normed,
        in_weight.reshape(features, heads_here * 3 * head_dim),
        preferred_element_type=jnp.float32,
    )
    mixed = mixed.reshape(group_size, stretch_max, heads_here, 3 * head_dim).astype(jnp.bfloat16)
    contexts = []
    for member in range(group_size):
        pairs = jnp.concatenate([current[member], mixed[member, :, :, head_dim:]], axis=0)
        contexts.append(
            attend(mixed[member, :, :, :head_dim], pairs, member_prefix[member], slopes, head_dim)
        )
    context = jnp.concatenate(contexts, axis=0)
    partial_attn = jnp.dot(
        context,
        out_weight.reshape(heads_here * head_dim, features),
        preferred_element_type=jnp.float32,
    )
    partial_attn = partial_attn.reshape(group_size, req_count, span_rows, features)
    attn_rows = lax.psum_scatter(
        partial_attn.astype(jnp.bfloat16), "head", scatter_dimension=2, tiled=True
    ).astype(jnp.float32)
    residual_rows = dealt_rows.astype(jnp.float32) + attn_rows
    normed_rows = layer_norm(residual_rows, mlp_gain).astype(jnp.bfloat16)
    normed_all = lax.all_gather(normed_rows, "head", axis=2, tiled=True)
    inner = jax.nn.gelu(
        jnp.dot(
            normed_all.reshape(group_size * stretch_max, features),
            up_weight,
            preferred_element_type=jnp.float32,
        ),
        approximate=False,
    ).astype(jnp.bfloat16)
    partial_mlp = jnp.dot(inner, down_weight, preferred_element_type=jnp.float32).reshape(
        group_size, req_count, span_rows, features
    )
    mlp_rows = lax.psum_scatter(
        partial_mlp.astype(jnp.bfloat16), "head", scatter_dimension=2, tiled=True
    ).astype(jnp.float32)
    row_number = (
        jnp.arange(req_count, dtype=jnp.int32)[:, None] * head_count + head_index
    ) * stretch_rows + jnp.arange(stretch_rows, dtype=jnp.int32)[None, :]
    usable = row_number[None] < member_stretch[:, None, None]
    result = jnp.where(
        usable[..., None], residual_rows + mlp_rows, jnp.zeros((), jnp.float32)
    ).astype(jnp.bfloat16)
    returned = lax.all_to_all(result, "req", split_axis=1, concat_axis=0, tiled=True).reshape(
        requests, stretch_rows, features
    )
    inverse = jnp.argsort(req_order)
    layer_out = jnp.take(returned, inverse, axis=0)
    return (layer_out, relaid)


def solution(mesh):
    return jax.shard_map(
        local,
        mesh=mesh,
        in_specs=(
            P(None, ("req", "head"), None),
            P("req", None, "head", None, None),
            P(),
            P(),
            P(),
            P(),
            P(None, "head", None),
            P("head"),
            P("head", None, None),
            P(),
            P(None, "head"),
            P("head", None),
        ),
        out_specs=(P(None, ("req", "head"), None), P(None, "req", None, "head", None)),
        check_vma=False,
    )
```

profile of v0, /device:TPU:1, one launch (start us, length us, event | category | flops | bytes accessed | tf_op | source)
XLA Modules:
  0.0 463.2 jit_solution(14605150824195133511)
XLA Ops:
  7.2 0.8 compare_select_fusion.1
  8.0 1.4 gather_fusion
  10.1 1.5 gather_fusion.3
  11.6 0.8 broadcast_select_fusion.1
  12.4 4.3 all-to-all-start
  16.7 5.3 %gather_fusion.1 = bf16[8,2,32,32,128]{4,3,2,1,0:T(8,128)(2,1)} fusion(bf16[2,8,32,32,128]{4,3,2,1,0:T(8,128)(2,1)} %param.17, s32[1024]{0:T(1024)S(1)} %pad_clamp_fusion.1), kind=kCustom, calls=%fused_computation.5 | custom fusion | bytes 8388640 | tf_op jit(solution)/shard_map/jit(_take)/gather | solution.py:81
  22.0 2.6 select_bitcast_fusion
  24.6 3.6 copy.44
  29.0 6.2 %all-to-all-start.1 = ((bf16[2,8,32,32,128]{4,2,0,1,3:T(8,128)(2,1)}), bf16[2,8,32,32,128]{4,2,0,1,3:T(8,128)(2,1)}, u32[]{:S(2)}, u32[]{:S(2)}) async-start(bf16[2,8,32,32,128]{4,2,0,1,3:T(8,128)(2,1)} %copy.44), calls=%async_computation.1 | async-start | bytes 8388608 | tf_op jit(solution)/shard_map/all_to_all | solution.py:85
  38.6 1.3 iota_compare_fusion.1
  41.2 112.4 %all-to-all-done.1 = bf16[2,8,32,32,128]{4,2,0,1,3:T(8,128)(2,1)} async-done(((bf16[2,8,32,32,128]{4,2,0,1,3:T(8,128)(2,1)}), bf16[2,8,32,32,128]{4,2,0,1,3:T(8,128)(2,1)}, u32[]{:S(2)}, u32[]{:S(2)}) %all-to-all-start.1) | async-done | bytes 4194336 | tf_op jit(solution)/shard_map/all_to_all | solution.py:85
  153.5 3.5 copy.46
  157.0 2.3 copy.47
  159.3 5.9 %all-to-all-start.2 = ((bf16[2,8,256,4,128]{4,2,3,0,1:T(8,128)(2,1)}), bf16[2,8,256,4,128]{4,2,3,0,1:T(8,128)(2,1)}, u32[]{:S(2)}, u32[]{:S(2)}) async-start(bf16[2,8,256,4,128]{4,2,3,0,1:T(8,128)(2,1)} %copy.47), calls=%async_computation.2 | async-start | bytes 8388608 | tf_op jit(solution)/shard_map/all_to_all | solution.py:84
  165.9 0.8 fusion.54
  166.7 1.0 subtract_convert_fusion.1
  167.6 0.9 subtract_convert_fusion
  168.6 2.1 convert_reduce_fusion
  171.5 0.7 fusion.6
  172.4 1.8 fusion.19
  174.2 0.9 copy-done.11
  175.1 37.5 %all-to-all-done.2 = bf16[2,8,256,4,128]{4,2,3,0,1:T(8,128)(2,1)} async-done(((bf16[2,8,256,4,128]{4,2,3,0,1:T(8,128)(2,1)}), bf16[2,8,256,4,128]{4,2,3,0,1:T(8,128)(2,1)}, u32[]{:S(2)}, u32[]{:S(2)}) %all-to-all-start.2) | async-done | bytes 4194336 | tf_op jit(solution)/shard_map/all_to_all | solution.py:84
  212.7 7.4 %copy.49 = bf16[4,2,2,256,4,128]{3,5,4,2,1,0:T(8,128)(2,1)} copy(bf16[4,2,2,256,4,128]{5,3,4,1,2,0:T(8,128)(2,1)} %bitcast.9) | data formatting | bytes 8388608 | tf_op jit(solution)/shard_map/all_to_all | solution.py:84
  220.1 1.1 slice_bitcast_fusion.3
  221.2 1.1 fusion.120
  222.2 1.9 convolution_convert_fusion.3
  224.1 1.1 fusion.119
  225.2 1.2 convolution_convert_fusion.2
  226.6 0.7 convolution_convert_fusion.1
  227.4 2.9 copy.74
  230.3 4.5 reshape.419
  235.5 63.5 %reduce-scatter.7.cloned.1.call-done = bf16[8,16384]{1,0:T(8,128)(2,1)} async-done(((bf16[64,16384]{1,0:T(8,128)(2,1)}), bf16[8,16384]{1,0:T(8,128)(2,1)}) %reduce-scatter.7.cloned.1.call-update) | async-done | bytes 262160
  299.0 1.1 reshape.420
  300.8 0.9 multiply_convert_fusion
  301.8 49.1 %all-gather.5.cloned.1.call-done = bf16[2,4,64,2048]{3,2,0,1:T(8,128)(2,1)} async-done(((bf16[2,4,8,2048]{3,2,0,1:T(8,128)(2,1)}), bf16[2,4,64,2048]{3,2,0,1:T(8,128)(2,1)}) %all-gather.5.cloned.1.call-update) | async-done | bytes 2097168 | tf_op jit(solution)/shard_map/all_gather | solution.py:126
  350.9 1.8 copy.53
  352.7 13.7 %convolution_convert_fusion = bf16[512,2048]{1,0:T(8,128)(2,1)} fusion(bf16[1024,2048]{1,0:T(8,128)(2,1)} %param.27, bf16[512,2048]{1,0:T(8,128)(2,1)S(1)} %bitcast.113, bf16[2048,1024]{1,0:T(8,128)(2,1)} %param.26), kind=kOutput, calls=%fused_computation.19 | convolution fusion | flops 4330094592 | bytes 12582912 | tf_op jit(solution)/shard_map/dot_general | solution.py:135
  366.4 3.2 copy.73
  369.6 2.8 reshape.421
  372.4 1.0 sort.17
  373.6 64.4 %reduce-scatter.9.cloned.1.call-done = bf16[8,16384]{1,0:T(8,128)(2,1)} async-done(((bf16[64,16384]{1,0:T(8,128)(2,1)}), bf16[8,16384]{1,0:T(8,128)(2,1)}) %reduce-scatter.9.cloned.1.call-update) | async-done | bytes 262160
  438.0 1.1 reshape.422
  439.1 1.0 select_convert_fusion
  440.2 5.9 %all-to-all-start.3 = ((bf16[2,4,8,2048]{3,2,0,1:T(8,128)(2,1)}), bf16[2,4,8,2048]{3,2,0,1:T(8,128)(2,1)S(1)}, u32[]{:S(2)}, u32[]{:S(2)}) async-start(bf16[2,4,8,2048]{3,2,0,1:T(8,128)(2,1)} %select_convert_fusion), calls=%async_computation.3 | async-start | bytes 524288 | tf_op jit(solution)/shard_map/all_to_all | solution.py:148
  446.1 7.6 %copy.55 = bf16[8,2,256,4,128]{4,3,2,1,0:T(4,128)(2,1)} copy(bf16[8,2,256,4,128]{2,4,3,1,0:T(8,128)(2,1)} %bitcast.101) | data formatting | bytes 8388608
  453.6 0.7 copy-done.7
  454.4 1.5 gather_fusion.5
  455.9 0.8 broadcast_select_fusion
  (83 shorter events, 9.6 us)
Async XLA Ops:
  7.2 165.2 %copy-start = (bf16[2048,4,192]{0,2,1:T(8,128)(2,1)S(1)}, bf16[2048,4,192]{0,2,1:T(8,128)(2,1)}, u32[]{:S(2)}) copy-start(bf16[2048,4,192]{0,2,1:T(8,128)(2,1)} %param.22) | copy-start | bytes 9437188
  12.4 15.8 %all-to-all-start = ((bf16[8,8,2048]{2,1,0:T(8,128)(2,1)}), bf16[8,8,2048]{2,1,0:T(8,128)(2,1)S(1)}, u32[]{:S(2)}, u32[]{:S(2)}) async-start(bf16[8,8,2048]{2,1,0:T(8,128)(2,1)} %broadcast_select_fusion.1), calls=%async_computation | async-start | bytes 524288 | tf_op jit(solution)/shard_map/all_to_all | solution.py:93
  28.2 7.6 %copy-start.17 = (s32[8]{0:T(128)S(1)}, s32[8]{0:T(128)}, u32[]{:S(2)}) copy-start(s32[8]{0:T(128)} %param.20) | copy-start | bytes 100
  28.2 7.7 %copy-start.2 = (s32[8]{0:T(128)S(1)}, s32[8]{0:T(128)}, u32[]{:S(2)}) copy-start(s32[8]{0:T(128)} %param.19) | copy-start | bytes 100
  28.2 8.4 %copy-start.3 = (s32[8]{0:T(128)S(1)}, s32[8]{0:T(128)}, u32[]{:S(2)}) copy-start(s32[8]{0:T(128)} %param.18) | copy-start | bytes 100
  28.2 9.0 %copy-start.15 = (bf16[2048]{0:T(1024)(128)(2,1)S(1)}, bf16[2048]{0:T(1024)(128)(2,1)}, u32[]{:S(2)}) copy-start(bf16[2048]{0:T(1024)(128)(2,1)} %param.21) | copy-start | bytes 12292
  28.3 0.7 copy-start.5
  29.0 124.6 %all-to-all-start.1 = ((bf16[2,8,32,32,128]{4,2,0,1,3:T(8,128)(2,1)}), bf16[2,8,32,32,128]{4,2,0,1,3:T(8,128)(2,1)}, u32[]{:S(2)}, u32[]{:S(2)}) async-start(bf16[2,8,32,32,128]{4,2,0,1,3:T(8,128)(2,1)} %copy.44), calls=%async_computation.1 | async-start | bytes 8388608 | tf_op jit(solution)/shard_map/all_to_all | solution.py:85
  35.1 133.5 %all-gather.3.cloned.1.call-start = ((), (), s32[]{:S(2)}) async-start(), calls=%async_computation.6 | async-start | bytes 2359296 | tf_op jit(solution)/shard_map/all_gather | solution.py:96
  159.3 53.4 %all-to-all-start.2 = ((bf16[2,8,256,4,128]{4,2,3,0,1:T(8,128)(2,1)}), bf16[2,8,256,4,128]{4,2,3,0,1:T(8,128)(2,1)}, u32[]{:S(2)}, u32[]{:S(2)}) async-start(bf16[2,8,256,4,128]{4,2,3,0,1:T(8,128)(2,1)} %copy.47), calls=%async_computation.2 | async-start | bytes 8388608 | tf_op jit(solution)/shard_map/all_to_all | solution.py:84
  165.3 133.7 %reduce-scatter.7.cloned.1.call-start = ((), (), s32[]{:S(2)}) async-start(), calls=%async_computation.8 | async-start | bytes 2359296
  168.6 2.2 copy-start.4
  174.2 0.9 copy-start.11
  212.7 8.5 %copy-start.10 = (f32[256,512]{1,0:T(8,128)S(1)}, f32[256,512]{1,0:T(8,128)}, u32[]{:S(2)}) copy-start(f32[256,512]{1,0:T(8,128)} %subtract_convert_fusion.1) | copy-start | bytes 1572868
  212.7 8.5 %copy-start.12 = (bf16[2,256,4,192]{1,3,2,0:T(8,128)(2,1)S(1)}, bf16[2,256,4,192]{1,3,2,0:T(8,128)(2,1)}, u32[]{:S(2)}) copy-start(bf16[2,256,4,192]{1,3,2,0:T(8,128)(2,1)} %copy-done.11) | copy-start | bytes 2359300
  212.7 8.5 %copy-start.13 = (pred[256,512]{1,0:T(8,128)(4,1)S(1)}, pred[256,512]{1,0:T(8,128)(4,1)}, u32[]{:S(2)}) copy-start(pred[256,512]{1,0:T(8,128)(4,1)} %get-tuple-element.24) | copy-start | bytes 393220
  212.7 8.5 %copy-start.18 = (f32[4]{0:T(128)S(1)}, f32[4]{0:T(128)}, u32[]{:S(2)}) copy-start(f32[4]{0:T(128)} %param.23) | copy-start | bytes 52
  222.2 1.9 copy-start.9
  225.2 1.3 copy-start.14
  225.2 1.4 copy-start.8
  234.8 0.7 copy-start.16
  234.8 65.4 %copy-start.6 = (bf16[8,8,2048]{2,1,0:T(8,128)(2,1)S(1)}, bf16[8,8,2048]{2,1,0:T(8,128)(2,1)}, u32[]{:S(2)}) copy-start(bf16[8,8,2048]{2,1,0:T(8,128)(2,1)} %copy-done.5) | copy-start | bytes 786436
  234.8 116.1 %all-gather.5.cloned.1.call-start = ((), (), s32[]{:S(2)}) async-start(), calls=%async_computation.7 | async-start | bytes 2359296 | tf_op jit(solution)/shard_map/all_gather | solution.py:126
  301.7 136.3 %reduce-scatter.9.cloned.1.call-start = ((), (), s32[]{:S(2)}) async-start(), calls=%async_computation.9 | async-start | bytes 2359296
  440.2 13.5 %all-to-all-start.3 = ((bf16[2,4,8,2048]{3,2,0,1:T(8,128)(2,1)}), bf16[2,4,8,2048]{3,2,0,1:T(8,128)(2,1)S(1)}, u32[]{:S(2)}, u32[]{:S(2)}) async-start(bf16[2,4,8,2048]{3,2,0,1:T(8,128)(2,1)} %select_convert_fusion), calls=%async_computation.3 | async-start | bytes 524288 | tf_op jit(solution)/shard_map/all_to_all | solution.py:148
  446.1 10.6 %copy-start.1 = (bf16[2048,4,192]{0,2,1:T(8,128)(2,1)S(1)}, bf16[2048,4,192]{0,2,1:T(8,128)(2,1)}, u32[]{:S(2)}) copy-start(bf16[2048,4,192]{0,2,1:T(8,128)(2,1)} %param.22) | copy-start | bytes 9437188
  453.6 0.7 copy-start.7
Sparse Core Ops, SparseCore 0:
  38.7 103.0 all-gather.2
  234.9 64.0 reduce-scatter.6
  301.9 49.0 all-gather.4
  372.6 65.4 reduce-scatter.8
where the time goes:
time: 464 us; the launch traced here: 463 us
  waiting for transfers between devices  328 us (71%)
  local copies, waits for them, and re-layouts  57.7 us (12%)
  starting transfers between devices  22.6 us (5%)
  matrix products  21.5 us (5%)
  other arithmetic  19.6 us (4%)
  between operations  14.1 us (3%)
    unnamed x6, waiting for transfers between devices  129 us
    all_to_all x1, waiting for transfers between devices, local(): lax.all_to_all(dealt_cache, 'head', split_axis=3, concat_axis=2, tiled=True)  112 us
    all_gather x1, waiting for transfers between devices, local(): normed_all = lax.all_gather(normed_rows, 'head', axis=2, tiled=True)  49.1 us
    all_to_all x1, waiting for transfers between devices, local(): lax.all_to_all(lax.all_to_all(dealt_cache, 'head', split_axis=3, concat_a...  37.5 us
    unnamed x45, local copies, waits for them, and re-layouts  26.1 us
    dot_general x1, matrix products, local(): jnp.dot(inner, down_weight, preferred_element_type=jnp.float32)  13.7 us
  transfers between devices with their start and end apart: 8, of which 5 were waited for; matrix products, arithmetic and copies ran while one was open for 9% of the time, Pallas kernels for 0%

commit v1 on v0

--- a/solution.py
+++ b/solution.py
@@ -5,6 +5,28 @@
 from jax.sharding import PartitionSpec as P
 
 EPSILON = 1e-05
+
+
+def in_blocks(x, dim, size):
+    before, after = (x.shape[:dim], x.shape[dim + 1 :])
+    return jnp.moveaxis(x.reshape(*before, size, -1, *after), dim, 0)
+
+
+def joined_along(blocks, dim):
+    blocks = jnp.moveaxis(blocks, 0, dim)
+    lengths = blocks.shape
+    return blocks.reshape(*lengths[:dim], lengths[dim] * lengths[dim + 1], *lengths[dim + 2 :])
+
+
+def exchange_in_pairs(x, axis, split_dim, concat_dim):
+    size, position = (lax.axis_size(axis), lax.axis_index(axis))
+    pieces = in_blocks(x, split_dim, size)
+    outs = [pieces[position]]
+    for hop in range(1, size):
+        sent = pieces[position ^ hop]
+        outs.append(lax.ppermute(sent, axis, [(i, i ^ hop) for i in range(size)]))
+    pieces = jnp.stack(outs)[position ^ jnp.arange(size)]
+    return joined_along(pieces, concat_dim)
 
 
 def layer_norm(values, gain):
@@ -82,11 +104,7 @@
         jnp.zeros((), cache_prefill.dtype),
     )
     relaid = lax.all_to_all(
-        lax.all_to_all(dealt_cache, "head", split_axis=3, concat_axis=2, tiled=True),
-        "req",
-        split_axis=1,
-        concat_axis=0,
-        tiled=True,
+        exchange_in_pairs(dealt_cache, "head", 3, 2), "req", split_axis=1, concat_axis=0, tiled=True
     )
     current = relaid[0]
     dealt_acts = jnp.take(stretch_acts, req_order, axis=0)

time: 464 us -> 474 us (1.022)
  waiting for transfers between devices: 328 us -> 299 us
  local copies, waits for them, and re-layouts: 57.7 us -> 75.9 us
  starting transfers between devices: 22.6 us -> 37.7 us
    all_to_all x2 -> x1, waiting for transfers between devices: 150 us -> 38.9 us  [local(): lax.all_to_all(exchange_in_pairs(dealt_cache, 'head', 3, 2), 'req', split...]
    ppermute x0 -> x7, waiting for transfers between devices: none -> 42.5 us  [exchange_in_pairs(): outs.append(lax.ppermute(sent, axis, [(i, i ^ hop) for i in range(size)]))]
    unnamed x6, waiting for transfers between devices: 129 us -> 165 us
    unnamed x45 -> x48, local copies, waits for them, and re-layouts: 26.1 us -> 38.9 us
    ppermute x0 -> x7, starting transfers between devices: none -> 11 us  [exchange_in_pairs(): outs.append(lax.ppermute(sent, axis, [(i, i ^ hop) for i in range(size)]))]
    all_to_all x3 -> x1, local copies, waits for them, and re-layouts: 13.1 us -> 7.26 us  [local(): lax.all_to_all(exchange_in_pairs(dealt_cache, 'head', 3, 2), 'req', split...]
    gather x0 -> x1, local copies, waits for them, and re-layouts: none -> 5.28 us  [exchange_in_pairs(): pieces = jnp.stack(outs)[position ^ jnp.arange(size)]]
    all_to_all x2 -> x1, starting transfers between devices: 12.1 us -> 15.2 us  [local(): lax.all_to_all(exchange_in_pairs(dealt_cache, 'head', 3, 2), 'req', split...]
  transfers between devices with their start and end apart: 8 -> 14, of which waited for: 5 -> 9; matrix products, arithmetic and copies ran while one was open for 9% -> 11% of each run, Pallas kernels for 0% -> 0%
where the time goes in v1:
time: 474 us; the launch traced here: 472 us
  waiting for transfers between devices  299 us (63%)
  local copies, waits for them, and re-layouts  75.9 us (16%)
  starting transfers between devices  37.7 us (8%)
  matrix products  25.1 us (5%)
  other arithmetic  20.8 us (4%)
  between operations  14.1 us (3%)
    unnamed x6, waiting for transfers between devices  165 us
    all_gather x1, waiting for transfers between devices, local(): normed_all = lax.all_gather(normed_rows, 'head', axis=2, tiled=True)  49 us
    ppermute x7, waiting for transfers between devices, exchange_in_pairs(): outs.append(lax.ppermute(sent, axis, [(i, i ^ hop) for i in range(size)]))  42.5 us
    unnamed x48, local copies, waits for them, and re-layouts  38.9 us
    all_to_all x1, waiting for transfers between devices, local(): lax.all_to_all(exchange_in_pairs(dealt_cache, 'head', 3, 2), 'req', split...  38.9 us
    all_to_all x1, starting transfers between devices, local(): lax.all_to_all(exchange_in_pairs(dealt_cache, 'head', 3, 2), 'req', split...  15.2 us
    dot_general x1, matrix products, local(): jnp.dot(inner, down_weight, preferred_element_type=jnp.float32)  13.7 us
    ppermute x7, starting transfers between devices, exchange_in_pairs(): outs.append(lax.ppermute(sent, axis, [(i, i ^ hop) for i in range(size)]))  11 us
  transfers between devices with their start and end apart: 14, of which 9 were waited for; matrix products, arithmetic and copies ran while one was open for 11% of the time, Pallas kernels for 0%

profile of v1, /device:TPU:1, one launch (start us, length us, event | category | flops | bytes accessed | tf_op | source)
XLA Modules:
  0.0 472.4 jit_solution(5484144538942857736)
XLA Ops:
  8.0 1.4 gather_fusion
  10.1 5.3 %gather_fusion.1 = bf16[8,2,32,32,128]{4,3,2,1,0:T(8,128)(2,1)} fusion(bf16[2,8,32,32,128]{4,3,2,1,0:T(8,128)(2,1)} %param.17, s32[1024]{0:T(1024)S(1)} %pad_clamp_fusion.2), kind=kCustom, calls=%fused_computation.5 | custom fusion | bytes 8388640 | tf_op jit(solution)/shard_map/jit(_take)/gather | solution.py:103
  15.5 3.8 fusion.7
  19.3 2.4 dynamic-slice_bitcast_fusion
  22.4 2.1 collective-permute-start
  24.5 1.3 collective-permute-start.1
  25.8 2.4 collective-permute-start.3
  29.2 1.5 gather_fusion.4
  31.5 5.4 %all-to-all-start = ((bf16[8,8,2048]{2,1,0:T(8,128)(2,1)}), bf16[8,8,2048]{2,1,0:T(8,128)(2,1)S(1)}, u32[]{:S(2)}, u32[]{:S(2)}) async-start(bf16[8,8,2048]{2,1,0:T(8,128)(2,1)} %broadcast_select_fusion.1), calls=%async_computation | async-start | bytes 524288 | tf_op jit(solution)/shard_map/all_to_all | solution.py:111
  37.0 1.9 bitcast_dynamic-update-slice_fusion.7
  38.9 3.4 all-to-all-done
  43.0 3.4 collective-permute-start.5
  46.4 1.9 bitcast_dynamic-update-slice_fusion.6
  48.3 14.1 %collective-permute-done.1 = bf16[2,8,32,4,128]{4,2,3,1,0:T(8,128)(2,1)} collective-permute-done((bf16[2,8,32,4,128]{4,2,3,1,0:T(8,128)(2,1)}, bf16[2,8,32,4,128]{4,2,3,1,0:T(8,128)(2,1)}, u32[]{:S(2)}, u32[]{:S(2)}) %collective-permute-start.1) | collective-permute-done | bytes 524320 | tf_op jit(solution)/shard_map/ppermute | solution.py:27
  63.2 1.9 bitcast_dynamic-update-slice_fusion.5
  65.0 9.8 %collective-permute-done.2 = bf16[2,8,32,4,128]{4,2,3,1,0:T(8,128)(2,1)} collective-permute-done((bf16[2,8,32,4,128]{4,2,3,1,0:T(8,128)(2,1)}, bf16[2,8,32,4,128]{4,2,3,1,0:T(8,128)(2,1)}, u32[]{:S(2)}, u32[]{:S(2)}) %collective-permute-start.2) | collective-permute-done | bytes 524320 | tf_op jit(solution)/shard_map/ppermute | solution.py:27
  74.8 1.9 bitcast_dynamic-update-slice_fusion.4
  76.7 1.9 bitcast_dynamic-update-slice_fusion.3
  78.6 1.9 bitcast_dynamic-update-slice_fusion.2
  80.5 8.3 %collective-permute-done.5 = bf16[2,8,32,4,128]{4,2,3,1,0:T(8,128)(2,1)S(1)} collective-permute-done((bf16[2,8,32,4,128]{4,2,3,1,0:T(8,128)(2,1)}, bf16[2,8,32,4,128]{4,2,3,1,0:T(8,128)(2,1)S(1)}, u32[]{:S(2)}, u32[]{:S(2)}) %collective-permute-start.5) | collective-permute-done | bytes 524320 | tf_op jit(solution)/shard_map/ppermute | solution.py:27
  89.7 10.2 %collective-permute-done.6 = bf16[2,8,32,4,128]{4,2,3,1,0:T(8,128)(2,1)S(1)} collective-permute-done((bf16[2,8,32,4,128]{4,2,3,1,0:T(8,128)(2,1)}, bf16[2,8,32,4,128]{4,2,3,1,0:T(8,128)(2,1)S(1)}, u32[]{:S(2)}, u32[]{:S(2)}) %collective-permute-start.6) | collective-permute-done | bytes 524320 | tf_op jit(solution)/shard_map/ppermute | solution.py:27
  100.8 5.3 %gather_fusion.2 = bf16[8,2,8,32,4,128]{5,3,4,2,1,0:T(8,128)(2,1)} fusion(bf16[8,2,8,32,4,128]{5,3,4,2,1,0:T(8,128)(2,1)} %bitcast_dynamic-update-slice_fusion, s32[1024]{0:T(1024)S(1)} %pad_clamp_fusion.1), kind=kCustom, calls=%fused_computation.6 | custom fusion | bytes 8388640 | tf_op jit(solution)/shard_map/gather | solution.py:28
  106.0 3.4 copy.38
  109.5 2.3 copy.39
  111.8 15.2 %all-to-all-start.1 = ((bf16[2,8,256,4,128]{4,2,3,0,1:T(8,128)(2,1)}), bf16[2,8,256,4,128]{4,2,3,0,1:T(8,128)(2,1)}, u32[]{:S(2)}, u32[]{:S(2)}) async-start(bf16[2,8,256,4,128]{4,2,3,0,1:T(8,128)(2,1)} %copy.39), calls=%async_computation.1 | async-start | bytes 8388608 | tf_op jit(solution)/shard_map/all_to_all | solution.py:106
  129.7 1.3 iota_compare_fusion.1
  135.4 38.9 %all-to-all-done.1 = bf16[2,8,256,4,128]{4,2,3,0,1:T(8,128)(2,1)} async-done(((bf16[2,8,256,4,128]{4,2,3,0,1:T(8,128)(2,1)}), bf16[2,8,256,4,128]{4,2,3,0,1:T(8,128)(2,1)}, u32[]{:S(2)}, u32[]{:S(2)}) %all-to-all-start.1) | async-done | bytes 4194336 | tf_op jit(solution)/shard_map/all_to_all | solution.py:106
  174.3 7.3 %copy.41 = bf16[4,2,2,256,4,128]{3,5,4,2,1,0:T(8,128)(2,1)} copy(bf16[4,2,2,256,4,128]{5,3,4,1,2,0:T(8,128)(2,1)} %bitcast.24) | data formatting | bytes 8388608 | tf_op jit(solution)/shard_map/all_to_all | solution.py:106
  181.6 1.8 slice_bitcast_fusion.3
  183.4 2.1 convert_reduce_fusion
  187.2 1.8 fusion.20
  189.9 2.3 fusion.122
  192.3 2.4 convolution_convert_fusion.3
  194.7 2.0 fusion.121
  196.7 2.2 convolution_convert_fusion.2
  199.8 2.9 copy.68
  202.8 4.5 reshape.464
  207.9 100.4 %reduce-scatter.7.cloned.1.call-done = bf16[8,16384]{1,0:T(8,128)(2,1)} async-done(((bf16[64,16384]{1,0:T(8,128)(2,1)}), bf16[8,16384]{1,0:T(8,128)(2,1)}) %reduce-scatter.7.cloned.1.call-update) | async-done | bytes 262160
  311.1 49.0 %all-gather.5.cloned.1.call-done = bf16[2,4,64,2048]{3,2,0,1:T(8,128)(2,1)} async-done(((bf16[2,4,8,2048]{3,2,0,1:T(8,128)(2,1)}), bf16[2,4,64,2048]{3,2,0,1:T(8,128)(2,1)}) %all-gather.5.cloned.1.call-update) | async-done | bytes 2097168 | tf_op jit(solution)/shard_map/all_gather | solution.py:144
  360.1 1.8 copy.45
  362.0 13.7 %convolution_convert_fusion = bf16[512,2048]{1,0:T(8,128)(2,1)} fusion(bf16[1024,2048]{1,0:T(8,128)(2,1)} %param.27, bf16[512,2048]{1,0:T(8,128)(2,1)S(1)} %bitcast.146, bf16[2048,1024]{1,0:T(8,128)(2,1)} %param.26), kind=kOutput, calls=%fused_computation.21 | convolution fusion | flops 4330094592 | bytes 12582912 | tf_op jit(solution)/shard_map/dot_general | solution.py:153
  375.6 3.2 copy.67
  378.8 2.8 reshape.466
  382.8 64.5 %reduce-scatter.9.cloned.1.call-done = bf16[8,16384]{1,0:T(8,128)(2,1)} async-done(((bf16[64,16384]{1,0:T(8,128)(2,1)}), bf16[8,16384]{1,0:T(8,128)(2,1)}) %reduce-scatter.9.cloned.1.call-update) | async-done | bytes 262160
  447.3 1.1 reshape.467
  449.4 5.8 %all-to-all-start.2 = ((bf16[2,4,8,2048]{3,2,0,1:T(8,128)(2,1)}), bf16[2,4,8,2048]{3,2,0,1:T(8,128)(2,1)S(1)}, u32[]{:S(2)}, u32[]{:S(2)}) async-start(bf16[2,4,8,2048]{3,2,0,1:T(8,128)(2,1)} %select_convert_fusion), calls=%async_computation.2 | async-start | bytes 524288 | tf_op jit(solution)/shard_map/all_to_all | solution.py:166
  455.2 7.6 %copy.47 = bf16[8,2,256,4,128]{4,3,2,1,0:T(4,128)(2,1)} copy(bf16[8,2,256,4,128]{2,4,3,1,0:T(8,128)(2,1)} %bitcast.132) | data formatting | bytes 8388608
  463.5 1.5 gather_fusion.6
  (102 shorter events, 25.1 us)
Async XLA Ops:
  7.2 180.0 %copy-start = (bf16[2048,4,192]{0,2,1:T(8,128)(2,1)S(1)}, bf16[2048,4,192]{0,2,1:T(8,128)(2,1)}, u32[]{:S(2)}) copy-start(bf16[2048,4,192]{0,2,1:T(8,128)(2,1)} %param.22) | copy-start | bytes 9437188
  19.3 3.1 copy-start.5
  22.4 20.6 %collective-permute-start = (bf16[2,8,32,4,128]{4,2,3,1,0:T(8,128)(2,1)}, bf16[2,8,32,4,128]{4,2,3,1,0:T(8,128)(2,1)}, u32[]{:S(2)}, u32[]{:S(2)}) collective-permute-start(bf16[2,8,32,4,128]{4,2,3,1,0:T(8,128)(2,1)} %get-tuple-element.26), channel_id=1, source_target_pairs={{0,1},{1,0},{2,3},{3,2},{4,5},{5,4},{6,7},{7,6},{8,9},{9,8},{10,11... | collective-permute-start | bytes 1572872 | tf_op jit(solution)/shard_map/ppermute | solution.py:27
  24.5 37.9 %collective-permute-start.1 = (bf16[2,8,32,4,128]{4,2,3,1,0:T(8,128)(2,1)}, bf16[2,8,32,4,128]{4,2,3,1,0:T(8,128)(2,1)}, u32[]{:S(2)}, u32[]{:S(2)}) collective-permute-start(bf16[2,8,32,4,128]{4,2,3,1,0:T(8,128)(2,1)} %get-tuple-element.25), channel_id=1, source_target_pairs={{0,2},{1,3},{2,0},{3,1},{4,6},{5,7},{6,4},{7,5},{8,10},{9,11},{10,... | collective-permute-start | bytes 1572872 | tf_op jit(solution)/shard_map/ppermute | solution.py:27
  25.8 49.0 %collective-permute-start.2 = (bf16[2,8,32,4,128]{4,2,3,1,0:T(8,128)(2,1)}, bf16[2,8,32,4,128]{4,2,3,1,0:T(8,128)(2,1)}, u32[]{:S(2)}, u32[]{:S(2)}) collective-permute-start(bf16[2,8,32,4,128]{4,2,3,1,0:T(8,128)(2,1)} %get-tuple-element.24), channel_id=1, source_target_pairs={{0,3},{1,2},{2,1},{3,0},{4,7},{5,6},{6,5},{7,4},{8,11},{9,10},{10,... | collective-permute-start | bytes 1572872 | tf_op jit(solution)/shard_map/ppermute | solution.py:27
  25.8 50.9 %collective-permute-start.3 = (bf16[2,8,32,4,128]{4,2,3,1,0:T(8,128)(2,1)}, bf16[2,8,32,4,128]{4,2,3,1,0:T(8,128)(2,1)}, u32[]{:S(2)}, u32[]{:S(2)}) collective-permute-start(bf16[2,8,32,4,128]{4,2,3,1,0:T(8,128)(2,1)} %get-tuple-element.23), channel_id=1, source_target_pairs={{0,4},{1,5},{2,6},{3,7},{4,0},{5,1},{6,2},{7,3},{8,12},{9,13},{10,... | collective-permute-start | bytes 1572872 | tf_op jit(solution)/shard_map/ppermute | solution.py:27
  28.2 50.4 %collective-permute-start.4 = (bf16[2,8,32,4,128]{4,2,3,1,0:T(8,128)(2,1)}, bf16[2,8,32,4,128]{4,2,3,1,0:T(8,128)(2,1)}, u32[]{:S(2)}, u32[]{:S(2)}) collective-permute-start(bf16[2,8,32,4,128]{4,2,3,1,0:T(8,128)(2,1)} %get-tuple-element.22), channel_id=1, source_target_pairs={{0,5},{1,4},{2,7},{3,6},{4,1},{5,0},{6,3},{7,2},{8,13},{9,12},{10,... | collective-permute-start | bytes 1572872 | tf_op jit(solution)/shard_map/ppermute | solution.py:27
  31.5 10.7 %all-to-all-start = ((bf16[8,8,2048]{2,1,0:T(8,128)(2,1)}), bf16[8,8,2048]{2,1,0:T(8,128)(2,1)S(1)}, u32[]{:S(2)}, u32[]{:S(2)}) async-start(bf16[8,8,2048]{2,1,0:T(8,128)(2,1)} %broadcast_select_fusion.1), calls=%async_computation | async-start | bytes 524288 | tf_op jit(solution)/shard_map/all_to_all | solution.py:111
  37.0 146.4 %all-gather.3.cloned.1.call-start = ((), (), s32[]{:S(2)}) async-start(), calls=%async_computation.5 | async-start | bytes 2359296 | tf_op jit(solution)/shard_map/all_gather | solution.py:114
  42.3 0.7 copy-start.6
  43.0 45.9 %collective-permute-start.5 = (bf16[2,8,32,4,128]{4,2,3,1,0:T(8,128)(2,1)}, bf16[2,8,32,4,128]{4,2,3,1,0:T(8,128)(2,1)S(1)}, u32[]{:S(2)}, u32[]{:S(2)}) collective-permute-start(bf16[2,8,32,4,128]{4,2,3,1,0:T(8,128)(2,1)} %get-tuple-element.21), channel_id=1, source_target_pairs={{0,6},{1,7},{2,4},{3,5},{4,2},{5,3},{6,0},{7,1},{8,14},{9,15},{10,... | collective-permute-start | bytes 1572872 | tf_op jit(solution)/shard_map/ppermute | solution.py:27
  62.3 37.6 %collective-permute-start.6 = (bf16[2,8,32,4,128]{4,2,3,1,0:T(8,128)(2,1)}, bf16[2,8,32,4,128]{4,2,3,1,0:T(8,128)(2,1)S(1)}, u32[]{:S(2)}, u32[]{:S(2)}) collective-permute-start(bf16[2,8,32,4,128]{4,2,3,1,0:T(8,128)(2,1)} %get-tuple-element.20), channel_id=1, source_target_pairs={{0,7},{1,6},{2,5},{3,4},{4,3},{5,2},{6,1},{7,0},{8,15},{9,14},{10,... | collective-permute-start | bytes 1572872 | tf_op jit(solution)/shard_map/ppermute | solution.py:27
  111.7 15.2 %copy-start.15 = (s32[8]{0:T(128)S(1)}, s32[8]{0:T(128)}, u32[]{:S(2)}) copy-start(s32[8]{0:T(128)} %param.20) | copy-start | bytes 100
  111.7 15.3 %copy-start.2 = (s32[8]{0:T(128)S(1)}, s32[8]{0:T(128)}, u32[]{:S(2)}) copy-start(s32[8]{0:T(128)} %param.19) | copy-start | bytes 100
  111.8 15.9 %copy-start.3 = (s32[8]{0:T(128)S(1)}, s32[8]{0:T(128)}, u32[]{:S(2)}) copy-start(s32[8]{0:T(128)} %param.18) | copy-start | bytes 100
  111.8 16.6 %copy-start.13 = (bf16[2048]{0:T(1024)(128)(2,1)S(1)}, bf16[2048]{0:T(1024)(128)(2,1)}, u32[]{:S(2)}) copy-start(bf16[2048]{0:T(1024)(128)(2,1)} %param.21) | copy-start | bytes 12292
  111.8 62.6 %all-to-all-start.1 = ((bf16[2,8,256,4,128]{4,2,3,0,1:T(8,128)(2,1)}), bf16[2,8,256,4,128]{4,2,3,0,1:T(8,128)(2,1)}, u32[]{:S(2)}, u32[]{:S(2)}) async-start(bf16[2,8,256,4,128]{4,2,3,0,1:T(8,128)(2,1)} %copy.39), calls=%async_computation.1 | async-start | bytes 8388608 | tf_op jit(solution)/shard_map/all_to_all | solution.py:106
  126.9 181.4 %reduce-scatter.7.cloned.1.call-start = ((), (), s32[]{:S(2)}) async-start(), calls=%async_computation.7 | async-start | bytes 2359296
  183.4 2.2 copy-start.4
  187.2 2.8 copy-start.16
  189.0 0.9 copy-start.11
  189.9 2.3 copy-start.12
  192.3 2.4 copy-start.10
  196.7 2.4 copy-start.9
  207.2 0.7 copy-start.14
  207.2 102.2 %copy-start.7 = (bf16[8,8,2048]{2,1,0:T(8,128)(2,1)S(1)}, bf16[8,8,2048]{2,1,0:T(8,128)(2,1)}, u32[]{:S(2)}) copy-start(bf16[8,8,2048]{2,1,0:T(8,128)(2,1)} %copy-done.6) | copy-start | bytes 786436
  207.2 152.9 %all-gather.5.cloned.1.call-start = ((), (), s32[]{:S(2)}) async-start(), calls=%async_computation.6 | async-start | bytes 2359296 | tf_op jit(solution)/shard_map/all_gather | solution.py:144
  311.0 136.3 %reduce-scatter.9.cloned.1.call-start = ((), (), s32[]{:S(2)}) async-start(), calls=%async_computation.8 | async-start | bytes 2359296
  449.4 13.4 %all-to-all-start.2 = ((bf16[2,4,8,2048]{3,2,0,1:T(8,128)(2,1)}), bf16[2,4,8,2048]{3,2,0,1:T(8,128)(2,1)S(1)}, u32[]{:S(2)}, u32[]{:S(2)}) async-start(bf16[2,4,8,2048]{3,2,0,1:T(8,128)(2,1)} %select_convert_fusion), calls=%async_computation.2 | async-start | bytes 524288 | tf_op jit(solution)/shard_map/all_to_all | solution.py:166
  455.2 10.6 %copy-start.1 = (bf16[2048,4,192]{0,2,1:T(8,128)(2,1)S(1)}, bf16[2048,4,192]{0,2,1:T(8,128)(2,1)}, u32[]{:S(2)}) copy-start(bf16[2048,4,192]{0,2,1:T(8,128)(2,1)} %param.22) | copy-start | bytes 9437188
  462.8 0.7 copy-start.8
Sparse Core Ops, SparseCore 0:
  43.1 99.5 all-gather.2
  207.4 100.8 reduce-scatter.6
  311.1 48.9 all-gather.4
  381.8 65.4 reduce-scatter.8
